TPU v7x, 32 devices: a whole 2x2x4 slice. The times are simulated.
32 devices in a mesh: parts: 2 (over y), tm: 4 (over x, core), cols: 4 (over z).
Axes of the slice: x: 2, y: 2, z: 4, core: 2. Of those that a mesh axis runs over, the one named last changes fastest.
Arguments:
- noise: float32 [16, 1024, 1024], P(('parts', 'tm'), None, 'cols'), parts along dimension 0, may hold values from -6 to 6
- inv_diag: float32 [16, 1024, 1024], P(('parts', 'tm'), None, 'cols'), parts along dimension 0, may hold values from -2 to 2, as said below
- coupling: float32 [16, 1024, 1024], P(('parts', 'tm'), None, 'cols'), parts along dimension 0, may hold values from -1 to 1, as said below
- order: int32 [1024], replicated, may hold values from 0 to 1023, each once
Outputs:
- sample: float32 [16, 1024, 1024], P(('parts', 'tm'), None, 'cols'), parts along dimension 0
There are 2 independent parts, one for each index of `parts`. A program takes and returns all parts, laid end to end along the dimension named above; an argument that names none is the same for every part. Nothing has to cross between parts.
Inputs may be any that keep to these rules, and one draw needn't show every extreme that they name: `order`: each of 0 to 1023 appears once. `inv_diag`: diagonal entries lie between 0.5 and 2, off-diagonal entries are small in magnitude. `coupling`: diagonal entries lie between 0.5 and 0.97, off-diagonal entries are small in magnitude.
All inputs are finite; a program needn't handle non-finite values.
Results may differ from a plain program's by a relative error of at most 0.00013.
Values sent between devices are 32-bit elements; how exact they have to be, the bound alone decides.
No kernel may reach another device: no remote copies, remote signals or barrier semaphores. Data moves between devices by JAX's collectives and lax.ppermute only.
A program may use at most 128 MiB of HBM per device.

v0:
```python
import jax
import jax.numpy as jnp
from jax import lax
from jax.sharding import PartitionSpec as P

low = jnp.bfloat16


def shifted(block, axis, distance):
    devices = range(lax.axis_size(axis))
    route = [(i - distance, i) for i in devices if i - distance in devices]
    return lax.ppermute(block, axis, route)


def split(value, count):
    parts = []
    rest = value
    for index in range(count):
        kept = lax.reduce_precision(rest, exponent_bits=8, mantissa_bits=7)
        parts.append(kept.astype(low))
        if index < count - 1:
            rest = rest - kept
    return parts


def bdot(left, right):
    return jnp.dot(left, right, preferred_element_type=jnp.float32)


def apply(matrix_parts, operand):
    high, small = matrix_parts
    operand_high, operand_small = split(operand, 2)
    return bdot(high, operand_high) + (bdot(high, operand_small) + bdot(small, operand_high))


def shards(noise, inv_diag, coupling, order):
    block_count = noise.shape[0]
    node_count = noise.shape[1]
    sample_count = noise.shape[2]
    pieces = 2 if sample_count % 256 == 0 else 1
    width = sample_count // pieces
    inv_full = lax.all_gather(inv_diag, "cols", axis=2, tiled=True)
    coupling_parts = [
        split(lax.all_gather(coupling[block], "cols", axis=1, tiled=True), 2)
        for block in range(block_count)
    ]
    driven = [apply(split(inv_full[block], 2), noise[block]) for block in range(block_count)]
    driven_pieces = [
        [driven[block][:, p * width : (p + 1) * width] for p in range(pieces)]
        for block in range(block_count)
    ]

    def chain(entering, piece, skip_last):
        carried = entering
        results = [None] * block_count
        for block in range(block_count - 1, -1, -1):
            if skip_last and block == block_count - 1:
                carried = driven_pieces[block][piece]
            else:
                carried = driven_pieces[block][piece] + apply(coupling_parts[block], carried)
            results[block] = carried
        return results

    first = [shifted(chain(None, p, True)[0], "tm", -1) for p in range(pieces)]

    def relay_step(step, entering):
        return [shifted(chain(entering[p], p, False)[0], "tm", -1) for p in range(pieces)]

    entering = lax.fori_loop(0, lax.axis_size("tm") - 2, relay_step, first)
    finals = [chain(entering[p], p, False) for p in range(pieces)]
    selector = (order[:, None] == jnp.arange(node_count, dtype=order.dtype)[None, :]).astype(low)
    outputs = []
    for block in range(block_count):
        field = jnp.concatenate([finals[p][block] for p in range(pieces)], axis=1)
        top, middle, bottom = split(field, 3)
        outputs.append(bdot(selector, top) + (bdot(selector, middle) + bdot(selector, bottom)))
    return jnp.stack(outputs, axis=0)


def solution(mesh):
    return jax.shard_map(
        shards,
        mesh=mesh,
        in_specs=(
            P(("parts", "tm"), None, "cols"),
            P(("parts", "tm"), None, "cols"),
            P(("parts", "tm"), None, "cols"),
            P(),
        ),
        out_specs=P(("parts", "tm"), None, "cols"),
        check_vma=False,
    )
```

profile of v0, /device:TPU:1, one launch (start us, length us, event | category | flops | bytes accessed | tf_op | source)
XLA Modules:
  0.0 439.5 jit_solution(6839977181822519246)
XLA Ops:
  6.5 3.0 fusion.150
  11.0 81.5 %all-gather.8.cloned.1.call-done = f32[1,1024,1024]{2,1,0:T(8,128)} async-done(((f32[1,1024,256]{2,1,0:T(8,128)}), f32[1,1024,1024]{2,1,0:T(8,128)}) %all-gather.8.cloned.1.call-update) | async-done | bytes 4194320 | tf_op jit(solution)/shard_map/all_gather | solution.py:44
  92.6 4.4 %reduce-precision_convert_fusion.13 = (bf16[1024,1024]{1,0:T(8,128)(2,1)S(1)}, bf16[1024,1024]{1,0:T(8,128)(2,1)}) fusion(f32[1,1024,1024]{2,1,0:T(8,128)} %all-gather.8.cloned.1.call-done), kind=kLoop, calls=%fused_computation.43 | loop fusion | flops 5242880 | bytes 8388608 | tf_op jit(solution)/shard_map/convert_element_type | solution.py:20
  97.0 76.5 %all-gather.10.cloned.1.call-done = f32[1,1024,1024]{2,1,0:T(8,128)} async-done(((f32[1,1024,256]{2,1,0:T(8,128)}), f32[1,1024,1024]{2,1,0:T(8,128)}) %all-gather.10.cloned.1.call-update) | async-done | bytes 4194320 | tf_op jit(solution)/shard_map/all_gather | solution.py:44
  173.5 5.0 %reduce-precision_convert_fusion.12 = (bf16[1024,1024]{1,0:T(8,128)(2,1)}, bf16[1024,1024]{1,0:T(8,128)(2,1)}) fusion(f32[1,1024,1024]{2,1,0:T(8,128)} %all-gather.10.cloned.1.call-done), kind=kLoop, calls=%fused_computation.41 | loop fusion | flops 5242880 | bytes 8388608 | tf_op jit(solution)/shard_map/convert_element_type | solution.py:20
  178.5 144.9 %all-gather.6.cloned.1.call-done = f32[2,1024,1024]{2,1,0:T(8,128)} async-done(((f32[2,1024,256]{2,1,0:T(8,128)}), f32[2,1024,1024]{2,1,0:T(8,128)}) %all-gather.6.cloned.1.call-update) | async-done | bytes 8388624 | tf_op jit(solution)/shard_map/all_gather | solution.py:42
  323.4 3.4 fusion.47
  326.9 3.8 fusion.97
  334.1 0.8 fusion.75
  334.9 0.8 fusion.72
  338.1 1.7 fusion.74
  339.8 1.7 fusion.71
  341.5 2.4 collective-permute-start.2
  343.8 2.1 collective-permute-start.3
  345.9 1.1 fusion.152
  347.0 2.0 copy.10
  349.0 2.0 copy.9
  351.1 2.3 fusion.151
  353.4 4.4 %collective-permute-done.3 = f32[1024,128]{0,1:T(8,128)S(1)} collective-permute-done((f32[1024,128]{0,1:T(8,128)}, f32[1024,128]{0,1:T(8,128)S(1)}, u32[]{:S(2)}, u32[]{:S(2)}) %collective-permute-start.3) | collective-permute-done | bytes 524320 | tf_op jit(solution)/shard_map/ppermute | solution.py:12
  357.8 54.2 %while.12 = (s32[]{:T(128)}, f32[1024,128]{0,1:T(8,128)S(1)}, f32[1024,128]{0,1:T(8,128)S(1)}, bf16[1024,1024]{1,0:T(8,128)(2,1)}, bf16[1024,1024]{1,0:T(8,128)(...) while((s32[]{:T(128)}, f32[1024,128]{0,1:T(8,128)S(1)}, ...), condition=%wide.region_1.0_spmd, body=%wide.region_0.0_spmd.sunk | while | flops 3226992640 | bytes 81789320 | solution.py:69
  357.8 2.5 fusion.228
  364.5 1.7 fusion.232
  366.2 1.9 collective-permute-start
  372.5 1.7 fusion.238
  374.2 1.9 collective-permute-start.1
  376.9 8.0 %collective-permute-done.1 = f32[1024,128]{0,1:T(8,128)S(1)} collective-permute-done((f32[1024,128]{0,1:T(8,128)}, f32[1024,128]{0,1:T(8,128)S(1)}, u32[]{:S(2)}, u32[]{:S(2)}) %collective-permute-start.1) | collective-permute-done | bytes 524320 | tf_op jit(solution)/shard_map/while/body/eval_jaxpr/ppermute | solution.py:12
  384.9 2.5 fusion.228
  391.7 1.7 fusion.232
  393.3 1.9 collective-permute-start
  399.7 1.7 fusion.238
  401.3 1.9 collective-permute-start.1
  404.0 8.0 %collective-permute-done.1 = f32[1024,128]{0,1:T(8,128)S(1)} collective-permute-done((f32[1024,128]{0,1:T(8,128)}, f32[1024,128]{0,1:T(8,128)S(1)}, u32[]{:S(2)}, u32[]{:S(2)}) %collective-permute-start.1) | collective-permute-done | bytes 524320 | tf_op jit(solution)/shard_map/while/body/eval_jaxpr/ppermute | solution.py:12
  412.0 2.6 fusion.136
  416.2 0.8 fusion.78
  417.4 0.8 fusion.77
  418.3 0.8 fusion.84
  419.1 0.8 fusion.83
  422.4 0.8 fusion.81
  423.6 0.8 fusion.80
  424.4 0.8 fusion.87
  425.3 0.8 fusion.86
  426.2 0.9 fusion.40
  427.0 0.9 fusion.43
  427.9 0.9 fusion.62
  428.8 0.9 fusion.61
  429.7 0.9 fusion.65
  430.6 0.9 fusion.64
  431.5 1.5 pad_maximum_fusion
  (86 shorter events, 30.6 us)
Async XLA Ops:
  6.5 86.0 %all-gather.8.cloned.1.call-start = ((), (), s32[]{:S(2)}) async-start(), calls=%async_computation.1 | async-start | bytes 5242880 | tf_op jit(solution)/shard_map/all_gather | solution.py:44
  9.6 163.9 %all-gather.10.cloned.1.call-start = ((), (), s32[]{:S(2)}) async-start(), calls=%async_computation.2 | async-start | bytes 5242880 | tf_op jit(solution)/shard_map/all_gather | solution.py:44
  10.3 313.1 %all-gather.6.cloned.1.call-start = ((), (), s32[]{:S(2)}) async-start(), calls=%async_computation | async-start | bytes 10485760 | tf_op jit(solution)/shard_map/all_gather | solution.py:42
  323.4 7.2 %copy-start.7 = (f32[2,1024,1024]{2,1,0:T(8,128)S(1)}, f32[2,1024,1024]{2,1,0:T(8,128)}, u32[]{:S(2)}) copy-start(f32[2,1024,1024]{2,1,0:T(8,128)} %all-gather.6.cloned.1.call-done) | copy-start | bytes 25165828
  326.8 4.0 copy-start.14
  330.8 1.6 copy-start.2
  331.6 14.3 %copy-start.8 = (f32[1024,256]{0,1:T(8,128)}, f32[1024,256]{0,1:T(8,128)S(1)}, u32[]{:S(2)}) copy-start(f32[1024,256]{0,1:T(8,128)S(1)} %fusion.69) | copy-start | bytes 3145732
  338.1 1.7 copy-start.15
  341.5 11.9 %collective-permute-start.2 = (f32[1024,128]{0,1:T(8,128)}, f32[1024,128]{0,1:T(8,128)S(1)}, u32[]{:S(2)}, u32[]{:S(2)}) collective-permute-start(f32[1024,128]{0,1:T(8,128)} %fusion.71), channel_id=1, source_target_pairs={{4,0},{8,4},{12,8},{5,1},{9,5},{13,9},{6,2},{10,6},{14,10},{7,3},{... | collective-permute-start | bytes 1572872 | tf_op jit(solution)/shard_map/ppermute | solution.py:12
  343.8 14.0 %collective-permute-start.3 = (f32[1024,128]{0,1:T(8,128)}, f32[1024,128]{0,1:T(8,128)S(1)}, u32[]{:S(2)}, u32[]{:S(2)}) collective-permute-start(f32[1024,128]{0,1:T(8,128)} %fusion.74), channel_id=1, source_target_pairs={{4,0},{8,4},{12,8},{5,1},{9,5},{13,9},{6,2},{10,6},{14,10},{7,3},{... | collective-permute-start | bytes 1572872 | tf_op jit(solution)/shard_map/ppermute | solution.py:12
  357.8 2.5 copy-start
  360.2 1.0 copy-start.11
  362.9 1.6 copy-start.3
  362.9 1.7 copy-start.13
  364.5 3.6 copy-start.5
  366.2 10.7 %collective-permute-start = (f32[1024,128]{0,1:T(8,128)}, f32[1024,128]{0,1:T(8,128)S(1)}, u32[]{:S(2)}, u32[]{:S(2)}) collective-permute-start(f32[1024,128]{0,1:T(8,128)} %fusion.232), channel_id=1, source_target_pairs={{4,0},{8,4},{12,8},{5,1},{9,5},{13,9},{6,2},{10,6},{14,10},{7,3},{... | collective-permute-start | bytes 1572872 | tf_op jit(solution)/shard_map/while/body/eval_jaxpr/ppermute | solution.py:12
  368.8 1.0 copy-start.10
  371.5 1.0 copy-start.12
  374.2 10.7 %collective-permute-start.1 = (f32[1024,128]{0,1:T(8,128)}, f32[1024,128]{0,1:T(8,128)S(1)}, u32[]{:S(2)}, u32[]{:S(2)}) collective-permute-start(f32[1024,128]{0,1:T(8,128)} %fusion.238), channel_id=1, source_target_pairs={{4,0},{8,4},{12,8},{5,1},{9,5},{13,9},{6,2},{10,6},{14,10},{7,3},{... | collective-permute-start | bytes 1572872 | tf_op jit(solution)/shard_map/while/body/eval_jaxpr/ppermute | solution.py:12
  384.9 2.5 copy-start
  387.4 1.0 copy-start.11
  390.0 1.6 copy-start.3
  390.0 1.7 copy-start.13
  391.6 3.6 copy-start.5
  393.3 10.7 %collective-permute-start = (f32[1024,128]{0,1:T(8,128)}, f32[1024,128]{0,1:T(8,128)S(1)}, u32[]{:S(2)}, u32[]{:S(2)}) collective-permute-start(f32[1024,128]{0,1:T(8,128)} %fusion.232), channel_id=1, source_target_pairs={{4,0},{8,4},{12,8},{5,1},{9,5},{13,9},{6,2},{10,6},{14,10},{7,3},{... | collective-permute-start | bytes 1572872 | tf_op jit(solution)/shard_map/while/body/eval_jaxpr/ppermute | solution.py:12
  396.0 1.0 copy-start.10
  398.6 1.0 copy-start.12
  401.3 10.7 %collective-permute-start.1 = (f32[1024,128]{0,1:T(8,128)}, f32[1024,128]{0,1:T(8,128)S(1)}, u32[]{:S(2)}, u32[]{:S(2)}) collective-permute-start(f32[1024,128]{0,1:T(8,128)} %fusion.238), channel_id=1, source_target_pairs={{4,0},{8,4},{12,8},{5,1},{9,5},{13,9},{6,2},{10,6},{14,10},{7,3},{... | collective-permute-start | bytes 1572872 | tf_op jit(solution)/shard_map/while/body/eval_jaxpr/ppermute | solution.py:12
  412.0 2.6 copy-start.6
  414.6 1.6 copy-start.1
  416.2 1.2 copy-start.9
  419.1 1.6 copy-start.4
  422.4 1.2 copy-start.16
  425.3 0.9 copy-start.17
Sparse Core Ops, SparseCore 0:
  9.7 82.8 all-gather.7
  94.1 79.2 all-gather.9
  175.0 148.3 all-gather.5
where the time goes:
time: 440 us; the launch traced here: 439 us
  waiting for transfers between devices  326 us (74%)
  matrix products  59.5 us (14%)
  local copies, waits for them, and re-layouts  16.8 us (4%)
  between operations  13.4 us (3%)
  starting transfers between devices  12.2 us (3%)
  other arithmetic  10.9 us (2%)
    all_gather x2, waiting for transfers between devices, shards(): lax.all_gather(coupling[block], 'cols', axis=1, tiled=True)  158 us
    all_gather x1, waiting for transfers between devices, shards(): inv_full = lax.all_gather(inv_diag, 'cols', axis=2, tiled=True)  145 us
    dot_general x54, matrix products, bdot(): return jnp.dot(left, right, preferred_element_type=jnp.float32)  59.5 us
    ppermute x6, waiting for transfers between devices, shifted(): return lax.ppermute(block, axis, route)  22 us
    ppermute x6, starting transfers between devices, shifted(): return lax.ppermute(block, axis, route)  12.1 us
    convert_element_type x2, other arithmetic, split(): parts.append(kept.astype(low))  9.48 us
  transfers between devices with their start and end apart: 9, of which 8 were waited for; matrix products, arithmetic and copies ran while one was open for 6% of the time, Pallas kernels for 0%

commit v1 on v0

--- a/solution.py
+++ b/solution.py
@@ -4,6 +4,27 @@
 from jax.sharding import PartitionSpec as P
 
 low = jnp.bfloat16
+
+
+def collect(x, axis, dim):
+    count, index, rows = (lax.axis_size(axis), lax.axis_index(axis), x.shape[dim])
+    right = [(i, (i + 1) % count) for i in range(count)]
+    downward = [(i, (i - 1) % count) for i in range(count)]
+    filled = jnp.zeros((*x.shape[:dim], count * rows, *x.shape[dim + 1 :]), x.dtype)
+    filled = lax.dynamic_update_slice_in_dim(filled, x, index * rows, axis=dim)
+    from_left = from_right = x
+    halfway = count // 2
+    for step in range(1, halfway + 1):
+        from_left = lax.ppermute(from_left, axis, right)
+        filled = lax.dynamic_update_slice_in_dim(
+            filled, from_left, (index - step) % count * rows, axis=dim
+        )
+        if step < count - halfway:
+            from_right = lax.ppermute(from_right, axis, downward)
+            filled = lax.dynamic_update_slice_in_dim(
+                filled, from_right, (index + step) % count * rows, axis=dim
+            )
+    return filled
 
 
 def shifted(block, axis, distance):
@@ -40,10 +61,7 @@
     pieces = 2 if sample_count % 256 == 0 else 1
     width = sample_count // pieces
     inv_full = lax.all_gather(inv_diag, "cols", axis=2, tiled=True)
-    coupling_parts = [
-        split(lax.all_gather(coupling[block], "cols", axis=1, tiled=True), 2)
-        for block in range(block_count)
-    ]
+    coupling_parts = [split(collect(coupling[block], "cols", 1), 2) for block in range(block_count)]
     driven = [apply(split(inv_full[block], 2), noise[block]) for block in range(block_count)]
     driven_pieces = [
         [driven[block][:, p * width : (p + 1) * width] for p in range(pieces)]

time: 440 us -> 404 us (0.918)
  waiting for transfers between devices: 326 us -> 208 us
  starting transfers between devices: 12.2 us -> 89.1 us
  local copies, waits for them, and re-layouts: 16.8 us -> 23.3 us
    ppermute x0 -> x6, waiting for transfers between devices: none -> 181 us  [the longest x4 137 us: collect(): from_left = lax.ppermute(from_left, axis, right)]
    all_gather x2 -> x0, waiting for transfers between devices: 158 us -> none  [shards(): lax.all_gather(coupling[block], 'cols', axis=1, tiled=True)]
    all_gather x1, waiting for transfers between devices: 145 us -> 6.52 us  [shards(): inv_full = lax.all_gather(inv_diag, 'cols', axis=2, tiled=True)]
    ppermute x0 -> x6, starting transfers between devices: none -> 77 us  [the longest x4 74.8 us: collect(): from_left = lax.ppermute(from_left, axis, right)]
    dynamic_update_slice x0 -> x7, local copies, waits for them, and re-layouts: none -> 4.76 us  [the longest x2 2.7 us: collect(): lax.dynamic_update_slice_in_dim(filled, from_right, (index + step) % coun...]
  transfers between devices with their start and end apart: 9 -> 13, of which waited for: 8 -> 11; matrix products, arithmetic and copies ran while one was open for 6% -> 8% of each run, Pallas kernels for 0% -> 0%
where the time goes in v1:
time: 404 us; the launch traced here: 400 us
  waiting for transfers between devices  208 us (51%)
  starting transfers between devices  89.1 us (22%)
  matrix products  59.4 us (15%)
  local copies, waits for them, and re-layouts  23.3 us (6%)
  between operations  13.8 us (3%)
  other arithmetic  6.7 us (2%)
    ppermute x4, waiting for transfers between devices, collect(): from_left = lax.ppermute(from_left, axis, right)  137 us
    ppermute x4, starting transfers between devices, collect(): from_left = lax.ppermute(from_left, axis, right)  74.8 us
    dot_general x54, matrix products, bdot(): return jnp.dot(left, right, preferred_element_type=jnp.float32)  59.4 us
    ppermute x2, waiting for transfers between devices, collect(): from_right = lax.ppermute(from_right, axis, downward)  44.3 us
    ppermute x6, waiting for transfers between devices, shifted(): return lax.ppermute(block, axis, route)  19.5 us
    ppermute x6, starting transfers between devices, shifted(): return lax.ppermute(block, axis, route)  12.1 us
  transfers between devices with their start and end apart: 13, of which 11 were waited for; matrix products, arithmetic and copies ran while one was open for 8% of the time, Pallas kernels for 0%

profile of v1, /device:TPU:1, one launch (start us, length us, event | category | flops | bytes accessed | tf_op | source)
XLA Modules:
  0.0 400.2 jit_solution(5640393190731548268)
XLA Ops:
  8.1 1.5 slice_bitcast_fusion.1
  9.6 2.1 collective-permute-start.2
  11.7 1.3 collective-permute-start.5
  13.0 2.0 collective-permute-start.3
  15.3 33.1 %collective-permute-done.2 = f32[1024,256]{1,0:T(8,128)S(1)} collective-permute-done((f32[1024,256]{1,0:T(8,128)}, f32[1024,256]{1,0:T(8,128)S(1)}, u32[]{:S(2)}, u32[]{:S(2)}) %collective-permute-start.2) | collective-permute-done | bytes 1048608 | tf_op jit(solution)/shard_map/ppermute | solution.py:18
  48.3 9.7 %collective-permute-start.4 = (f32[1024,256]{1,0:T(8,128)S(1)}, f32[1024,256]{1,0:T(8,128)S(1)}, u32[]{:S(2)}, u32[]{:S(2)}) collective-permute-start(f32[1024,256]{1,0:T(8,128)S(1)} %collective-permute-done.2), channel_id=1, source_target_pairs={{0,1},{1,2},{2,3},{3,0},{4,5},{5,6},{6,7},{7,4},{8,9},{9,10},{10,1... | collective-permute-start | bytes 3145736 | tf_op jit(solution)/shard_map/ppermute | solution.py:18
  58.0 35.3 %collective-permute-done.5 = f32[1024,256]{1,0:T(8,128)} collective-permute-done((f32[1024,256]{1,0:T(8,128)}, f32[1024,256]{1,0:T(8,128)}, u32[]{:S(2)}, u32[]{:S(2)}) %collective-permute-start.5) | collective-permute-done | bytes 1048608 | tf_op jit(solution)/shard_map/ppermute | solution.py:18
  93.4 61.7 %collective-permute-start.7 = (f32[1024,256]{1,0:T(8,128)}, f32[1024,256]{1,0:T(8,128)S(1)}, u32[]{:S(2)}, u32[]{:S(2)}) collective-permute-start(f32[1024,256]{1,0:T(8,128)} %collective-permute-done.5), channel_id=1, source_target_pairs={{0,1},{1,2},{2,3},{3,0},{4,5},{5,6},{6,7},{7,4},{8,9},{9,10},{10,1... | collective-permute-start | bytes 3145736 | tf_op jit(solution)/shard_map/ppermute | solution.py:18
  156.5 1.4 constant_dynamic-update-slice_fusion.2
  157.9 1.4 constant_dynamic-update-slice_fusion.5
  159.2 44.3 %collective-permute-done.6 = f32[1024,256]{1,0:T(8,128)} collective-permute-done((f32[1024,256]{1,0:T(8,128)}, f32[1024,256]{1,0:T(8,128)}, u32[]{:S(2)}, u32[]{:S(2)}) %collective-permute-start.6) | collective-permute-done | bytes 1048608 | tf_op jit(solution)/shard_map/ppermute | solution.py:23
  203.5 1.3 constant_dynamic-update-slice_fusion.1
  204.8 23.3 %collective-permute-done.4 = f32[1024,256]{1,0:T(8,128)S(1)} collective-permute-done((f32[1024,256]{1,0:T(8,128)S(1)}, f32[1024,256]{1,0:T(8,128)S(1)}, u32[]{:S(2)}, u32[]{:S(2)}) %collective-permute-start.4) | collective-permute-done | bytes 1048608 | tf_op jit(solution)/shard_map/ppermute | solution.py:18
  228.1 44.9 %collective-permute-done.7 = f32[1024,256]{1,0:T(8,128)S(1)} collective-permute-done((f32[1024,256]{1,0:T(8,128)}, f32[1024,256]{1,0:T(8,128)S(1)}, u32[]{:S(2)}, u32[]{:S(2)}) %collective-permute-start.7) | collective-permute-done | bytes 1048608 | tf_op jit(solution)/shard_map/ppermute | solution.py:18
  273.4 2.3 reduce-precision_convert_fusion.14
  275.6 3.0 reduce-precision_convert_fusion.12
  278.6 6.5 %all-gather.2.cloned.1.call-done = f32[2,1024,1024]{2,1,0:T(8,128)} async-done(((f32[2,1024,256]{2,1,0:T(8,128)}), f32[2,1024,1024]{2,1,0:T(8,128)}) %all-gather.2.cloned.1.call-update) | async-done | bytes 8388624 | tf_op jit(solution)/shard_map/all_gather | solution.py:63
  285.1 3.4 fusion.47
  288.6 3.8 fusion.85
  299.0 1.7 fusion.74
  300.6 2.3 collective-permute-start.9
  303.9 1.6 fusion.75
  305.5 2.1 collective-permute-start.8
  307.6 1.0 fusion.139
  308.6 2.1 copy.13
  310.7 2.0 copy.14
  312.7 2.3 fusion.138
  315.0 1.9 collective-permute-done.8
  317.0 55.5 %while.12 = (s32[]{:T(128)}, f32[1024,128]{0,1:T(8,128)S(1)}, f32[1024,128]{0,1:T(8,128)S(1)}, bf16[1024,1024]{1,0:T(8,128)(2,1)}, bf16[1024,1024]{1,0:T(8,128)(...) while((s32[]{:T(128)}, f32[1024,128]{0,1:T(8,128)S(1)}, ...), condition=%wide.region_1.2_spmd, body=%wide.region_0.1_spmd.sunk | while | flops 3226992640 | bytes 81789320 | solution.py:87
  317.0 2.5 fusion.220
  324.3 1.7 fusion.225
  326.0 1.9 collective-permute-start.1
  332.3 1.6 fusion.219
  334.0 1.9 collective-permute-start
  336.7 8.0 %collective-permute-done = f32[1024,128]{0,1:T(8,128)S(1)} collective-permute-done((f32[1024,128]{0,1:T(8,128)}, f32[1024,128]{0,1:T(8,128)S(1)}, u32[]{:S(2)}, u32[]{:S(2)}) %collective-permute-start) | collective-permute-done | bytes 524320 | tf_op jit(solution)/shard_map/while/body/eval_jaxpr/ppermute | solution.py:33
  344.7 2.5 fusion.220
  352.1 1.7 fusion.225
  353.8 1.9 collective-permute-start.1
  360.1 1.6 fusion.219
  361.7 1.9 collective-permute-start
  364.5 8.0 %collective-permute-done = f32[1024,128]{0,1:T(8,128)S(1)} collective-permute-done((f32[1024,128]{0,1:T(8,128)}, f32[1024,128]{0,1:T(8,128)S(1)}, u32[]{:S(2)}, u32[]{:S(2)}) %collective-permute-start) | collective-permute-done | bytes 524320 | tf_op jit(solution)/shard_map/while/body/eval_jaxpr/ppermute | solution.py:33
  372.5 2.6 fusion.122
  386.5 0.9 fusion.40
  388.3 0.9 fusion.62
  389.2 0.9 fusion.61
  390.1 0.9 fusion.65
  391.0 0.9 fusion.64
  391.9 1.5 pad_maximum_fusion
  (103 shorter events, 43.3 us)
Async XLA Ops:
  6.5 1.6 copy-start.17
  6.5 278.6 %all-gather.2.cloned.1.call-start = ((), (), s32[]{:S(2)}) async-start(), calls=%async_computation | async-start | bytes 10485760 | tf_op jit(solution)/shard_map/all_gather | solution.py:63
  9.6 38.7 %collective-permute-start.2 = (f32[1024,256]{1,0:T(8,128)}, f32[1024,256]{1,0:T(8,128)S(1)}, u32[]{:S(2)}, u32[]{:S(2)}) collective-permute-start(f32[1024,256]{1,0:T(8,128)} %get-tuple-element.102), channel_id=1, source_target_pairs={{0,1},{1,2},{2,3},{3,0},{4,5},{5,6},{6,7},{7,4},{8,9},{9,10},{10,1... | collective-permute-start | bytes 3145736 | tf_op jit(solution)/shard_map/ppermute | solution.py:18
  11.7 81.7 %collective-permute-start.5 = (f32[1024,256]{1,0:T(8,128)}, f32[1024,256]{1,0:T(8,128)}, u32[]{:S(2)}, u32[]{:S(2)}) collective-permute-start(f32[1024,256]{1,0:T(8,128)} %get-tuple-element.103), channel_id=1, source_target_pairs={{0,1},{1,2},{2,3},{3,0},{4,5},{5,6},{6,7},{7,4},{8,9},{9,10},{10,1... | collective-permute-start | bytes 3145736 | tf_op jit(solution)/shard_map/ppermute | solution.py:18
  13.0 144.8 %collective-permute-start.3 = (f32[1024,256]{1,0:T(8,128)}, f32[1024,256]{1,0:T(8,128)}, u32[]{:S(2)}, u32[]{:S(2)}) collective-permute-start(f32[1024,256]{1,0:T(8,128)} %get-tuple-element.102), channel_id=1, source_target_pairs={{0,3},{1,0},{2,1},{3,2},{4,7},{5,4},{6,5},{7,6},{8,11},{9,8},{10,9... | collective-permute-start | bytes 3145736 | tf_op jit(solution)/shard_map/ppermute | solution.py:23
  15.0 188.5 %collective-permute-start.6 = (f32[1024,256]{1,0:T(8,128)}, f32[1024,256]{1,0:T(8,128)}, u32[]{:S(2)}, u32[]{:S(2)}) collective-permute-start(f32[1024,256]{1,0:T(8,128)} %get-tuple-element.103), channel_id=1, source_target_pairs={{0,3},{1,0},{2,1},{3,2},{4,7},{5,4},{6,5},{7,6},{8,11},{9,8},{10,9... | collective-permute-start | bytes 3145736 | tf_op jit(solution)/shard_map/ppermute | solution.py:23
  48.3 179.8 %collective-permute-start.4 = (f32[1024,256]{1,0:T(8,128)S(1)}, f32[1024,256]{1,0:T(8,128)S(1)}, u32[]{:S(2)}, u32[]{:S(2)}) collective-permute-start(f32[1024,256]{1,0:T(8,128)S(1)} %collective-permute-done.2), channel_id=1, source_target_pairs={{0,1},{1,2},{2,3},{3,0},{4,5},{5,6},{6,7},{7,4},{8,9},{9,10},{10,1... | collective-permute-start | bytes 3145736 | tf_op jit(solution)/shard_map/ppermute | solution.py:18
  93.4 179.7 %collective-permute-start.7 = (f32[1024,256]{1,0:T(8,128)}, f32[1024,256]{1,0:T(8,128)S(1)}, u32[]{:S(2)}, u32[]{:S(2)}) collective-permute-start(f32[1024,256]{1,0:T(8,128)} %collective-permute-done.5), channel_id=1, source_target_pairs={{0,1},{1,2},{2,3},{3,0},{4,5},{5,6},{6,7},{7,4},{8,9},{9,10},{10,1... | collective-permute-start | bytes 3145736 | tf_op jit(solution)/shard_map/ppermute | solution.py:18
  285.1 7.2 %copy-start.7 = (f32[2,1024,1024]{2,1,0:T(8,128)S(1)}, f32[2,1024,1024]{2,1,0:T(8,128)}, u32[]{:S(2)}) copy-start(f32[2,1024,1024]{2,1,0:T(8,128)} %all-gather.2.cloned.1.call-done) | copy-start | bytes 25165828
  288.5 4.0 copy-start.14
  292.5 1.6 copy-start.2
  293.3 14.3 %copy-start.8 = (f32[1024,256]{0,1:T(8,128)}, f32[1024,256]{0,1:T(8,128)S(1)}, u32[]{:S(2)}) copy-start(f32[1024,256]{0,1:T(8,128)S(1)} %fusion.69) | copy-start | bytes 3145732
  299.0 4.9 %copy-start.15 = (f32[1024,256]{0,1:T(8,128)}, f32[1024,256]{0,1:T(8,128)S(1)}, u32[]{:S(2)}) copy-start(f32[1024,256]{0,1:T(8,128)S(1)} %fusion.67) | copy-start | bytes 3145732
  300.6 14.4 %collective-permute-start.9 = (f32[1024,128]{0,1:T(8,128)}, f32[1024,128]{0,1:T(8,128)S(1)}, u32[]{:S(2)}, u32[]{:S(2)}) collective-permute-start(f32[1024,128]{0,1:T(8,128)} %fusion.74), channel_id=1, source_target_pairs={{4,0},{8,4},{12,8},{5,1},{9,5},{13,9},{6,2},{10,6},{14,10},{7,3},{... | collective-permute-start | bytes 1572872 | tf_op jit(solution)/shard_map/ppermute | solution.py:33
  305.5 11.5 %collective-permute-start.8 = (f32[1024,128]{0,1:T(8,128)}, f32[1024,128]{0,1:T(8,128)S(1)}, u32[]{:S(2)}, u32[]{:S(2)}) collective-permute-start(f32[1024,128]{0,1:T(8,128)} %fusion.75), channel_id=1, source_target_pairs={{4,0},{8,4},{12,8},{5,1},{9,5},{13,9},{6,2},{10,6},{14,10},{7,3},{... | collective-permute-start | bytes 1572872 | tf_op jit(solution)/shard_map/ppermute | solution.py:33
  317.0 2.5 copy-start.5
  319.4 1.6 copy-start
  319.4 1.7 copy-start.11
  322.7 1.6 copy-start.3
  322.7 1.7 copy-start.12
  326.0 10.7 %collective-permute-start.1 = (f32[1024,128]{0,1:T(8,128)}, f32[1024,128]{0,1:T(8,128)S(1)}, u32[]{:S(2)}, u32[]{:S(2)}) collective-permute-start(f32[1024,128]{0,1:T(8,128)} %fusion.225), channel_id=1, source_target_pairs={{4,0},{8,4},{12,8},{5,1},{9,5},{13,9},{6,2},{10,6},{14,10},{7,3},{... | collective-permute-start | bytes 1572872 | tf_op jit(solution)/shard_map/while/body/eval_jaxpr/ppermute | solution.py:33
  328.6 1.0 copy-start.10
  331.3 1.0 copy-start.13
  334.0 10.7 %collective-permute-start = (f32[1024,128]{0,1:T(8,128)}, f32[1024,128]{0,1:T(8,128)S(1)}, u32[]{:S(2)}, u32[]{:S(2)}) collective-permute-start(f32[1024,128]{0,1:T(8,128)} %fusion.219), channel_id=1, source_target_pairs={{4,0},{8,4},{12,8},{5,1},{9,5},{13,9},{6,2},{10,6},{14,10},{7,3},{... | collective-permute-start | bytes 1572872 | tf_op jit(solution)/shard_map/while/body/eval_jaxpr/ppermute | solution.py:33
  344.7 2.5 copy-start.5
  347.2 1.6 copy-start
  347.2 1.7 copy-start.11
  350.4 1.6 copy-start.3
  350.4 1.7 copy-start.12
  353.8 10.7 %collective-permute-start.1 = (f32[1024,128]{0,1:T(8,128)}, f32[1024,128]{0,1:T(8,128)S(1)}, u32[]{:S(2)}, u32[]{:S(2)}) collective-permute-start(f32[1024,128]{0,1:T(8,128)} %fusion.225), channel_id=1, source_target_pairs={{4,0},{8,4},{12,8},{5,1},{9,5},{13,9},{6,2},{10,6},{14,10},{7,3},{... | collective-permute-start | bytes 1572872 | tf_op jit(solution)/shard_map/while/body/eval_jaxpr/ppermute | solution.py:33
  356.4 1.0 copy-start.10
  359.1 1.0 copy-start.13
  361.7 10.7 %collective-permute-start = (f32[1024,128]{0,1:T(8,128)}, f32[1024,128]{0,1:T(8,128)S(1)}, u32[]{:S(2)}, u32[]{:S(2)}) collective-permute-start(f32[1024,128]{0,1:T(8,128)} %fusion.219), channel_id=1, source_target_pairs={{4,0},{8,4},{12,8},{5,1},{9,5},{13,9},{6,2},{10,6},{14,10},{7,3},{... | collective-permute-start | bytes 1572872 | tf_op jit(solution)/shard_map/while/body/eval_jaxpr/ppermute | solution.py:33
  372.5 2.6 copy-start.1
  375.0 1.2 copy-start.9
  376.3 1.6 copy-start.4
  378.7 1.2 copy-start.16
  379.9 1.6 copy-start.6
  385.7 0.9 copy-start.18
Sparse Core Ops, SparseCore 0:
  8.9 276.1 all-gather.1
